TPU v7x, 32 devices: a whole 2x2x4 slice. The times are simulated.
32 devices in a mesh: illum: 8 (over z, y), tile: 4 (over x, core).
Axes of the slice: x: 2, y: 2, z: 4, core: 2. Of those that a mesh axis runs over, the one named last changes fastest.
Arguments:
- tilts: int32 [8, 2], P('illum'), may hold values from -64 to 64
- taps: float32 [2, 33], replicated, may hold values from -0.75 to 0.75
- stored_planes: float32 [2, 128, 4096], P(None, 'tile', 'illum'), may hold values from -3.140625 to 3.140625
- owner: int32 [2, 8], replicated, may hold values from 0 to 7, each once within a row
Outputs:
- exit_field: float32 [2, 8, 128, 4096], P(None, 'illum', 'tile')
Inputs may be any that keep to these rules, and one draw needn't show every extreme that they name: Each row of owner is a permutation of the 8 stored column blocks.
All inputs are finite; a program needn't handle non-finite values.
Results may differ from a plain program's by a relative error of at most 0.0003.
Values sent between devices are 32-bit elements; how exact they have to be, the bound alone decides.
No kernel may reach another device: no remote copies, remote signals or barrier semaphores. Data moves between devices by JAX's collectives and lax.ppermute only.
A program may use at most 64 MiB of HBM per device.

v0:
```python
import jax
import jax.numpy as jnp
from jax import lax
from jax.sharding import PartitionSpec as P

NY = 4096
PLANES = 2
HALF = 16
two_pi = 6.283185307179586


def extended(cells, sides, width):
    for axis, dim in sides:
        count = lax.axis_size(axis)
        ends = count - 1
        head = lax.slice_in_dim(cells, 0, width, axis=dim)
        tail = lax.slice_in_dim(cells, cells.shape[dim] - width, cells.shape[dim], axis=dim)
        cells = jnp.concatenate(
            [
                lax.ppermute(tail, axis, [(i, (i + 1) % count) for i in range(ends)]),
                cells,
                lax.ppermute(head, axis, [((i + 1) % count, i) for i in range(ends)]),
            ],
            axis=dim,
        )
    return cells


def toeplitz(tap_row, block):
    rows = jnp.arange(block + 2 * HALF)[:, None]
    cols = jnp.arange(block)[None, :]
    offset = rows - cols
    steps = jnp.arange(2 * HALF + 1)
    return jnp.sum(jnp.where(offset[:, :, None] == steps, tap_row, 0.0), axis=2)


def band_matrix(tap_row, count):
    rows = jnp.arange(count)[:, None]
    cols = jnp.arange(count + 2 * HALF)[None, :]
    offset = cols - rows
    steps = jnp.arange(2 * HALF + 1)
    return jnp.sum(jnp.where(offset[:, :, None] == steps, tap_row, 0.0), axis=2)


def windows(field, block):
    length = field.shape[-1]
    count = length // block
    widths = [(0, 0)] * (field.ndim - 1) + [(HALF, block - HALF)]
    padded = jnp.pad(field, widths)
    lead = field.shape[:-1]
    main = padded[..., :length].reshape(lead + (count, block))
    after = padded[..., block : length + block].reshape(lead + (count, block))[..., : 2 * HALF]
    return jnp.concatenate([main, after], axis=-1)


def along_pass(real, imag, taps):
    block = min(128, real.shape[-1])
    win_real = windows(real, block)
    win_imag = windows(imag, block)
    kern_real = toeplitz(taps[0], block)
    kern_imag = toeplitz(taps[1], block)

    def apply(win, kern):
        out = jnp.einsum("...nj,jc->...nc", win, kern, precision=lax.Precision.HIGHEST)
        return out.reshape(real.shape)

    return (
        apply(win_real, kern_real) - apply(win_imag, kern_imag),
        apply(win_real, kern_imag) + apply(win_imag, kern_real),
    )


def cross_pass(real, imag, taps):
    count = real.shape[1] - 2 * HALF
    band_real = band_matrix(taps[0], count)
    band_imag = band_matrix(taps[1], count)

    def apply(band, field):
        return jnp.einsum("ij,ajy->aiy", band, field, precision=lax.Precision.HIGHEST)

    return (
        apply(band_real, real) - apply(band_imag, imag),
        apply(band_real, imag) + apply(band_imag, real),
    )


def transmit(real, imag, screen):
    cosine = jnp.cos(screen)
    sine = jnp.sin(screen)
    return (real * cosine - imag * sine, real * sine + imag * cosine)


def reorder(gathered, owner):
    count = gathered.shape[1]
    blocks = owner.shape[1]
    width = gathered.shape[2] // blocks
    planes = [
        gathered[p].reshape(count, blocks, width)[:, owner[p], :].reshape(count, blocks * width)
        for p in range(gathered.shape[0])
    ]
    return jnp.stack(planes)


def body(tilts, taps, stored_planes, owner):
    local_rows = stored_planes.shape[1]
    total_rows = local_rows * lax.axis_size("tile")
    total_cols = NY
    first_row = lax.axis_index("tile") * local_rows
    gathered = lax.all_gather(stored_planes, "illum", axis=2, tiled=True)
    screens = reorder(gathered, owner)
    extra = 0
    span = local_rows + 2 * extra
    global_rows = first_row - extra + jnp.arange(span, dtype=jnp.int32)
    inside = (global_rows >= 0) & (global_rows < total_rows)
    cols = jnp.arange(total_cols, dtype=jnp.int32)
    across = (
        jnp.mod(tilts[:, 0:1] * global_rows[None, :], total_rows).astype(jnp.float32) / total_rows
    )
    along = jnp.mod(tilts[:, 1:2] * cols[None, :], total_cols).astype(jnp.float32) / total_cols
    theta = two_pi * (across[:, :, None] + along[:, None, :])
    real = jnp.where(inside[None, :, None], jnp.cos(theta), 0.0)
    imag = jnp.where(inside[None, :, None], jnp.sin(theta), 0.0)
    for plane in range(PLANES):
        real, imag = transmit(real, imag, screens[plane])
        packed = extended(jnp.stack([real, imag]), (("tile", 2),), HALF)
        real, imag = cross_pass(packed[0], packed[1], taps)
        real, imag = along_pass(real, imag, taps)
    return jnp.stack([real, imag])


def solution(mesh):
    in_specs = (P("illum", None), P(), P(None, "tile", "illum"), P())
    out_specs = P(None, "illum", "tile", None)
    return jax.shard_map(body, mesh=mesh, in_specs=in_specs, out_specs=out_specs, check_vma=False)
```

profile of v0, /device:TPU:1, one launch (start us, length us, event | category | flops | bytes accessed | tf_op | source)
XLA Modules:
  0.0 116.0 jit_solution(4339684245039347680)
XLA Ops:
  6.5 0.7 all-gather.2.cloned.1.call-update
  7.3 1.4 %fusion.42 = (s32[1,1]{1,0:T(1,128)}, s32[1,1]{1,0:T(1,128)}) fusion(s32[1,2]{1,0:T(1,128)} %param.4), kind=kLoop, calls=%fused_computation.110 | loop fusion | bytes 16 | tf_op jit(solution)/shard_map/slice | solution.py:117
  9.3 0.8 fusion.32
  10.1 0.7 fusion.24
  10.8 0.8 slice_bitcast_fusion.20
  11.8 39.1 %all-gather.2.cloned.1.call-done = f32[2,32,4096]{2,1,0:T(8,128)} async-done(((f32[2,32,512]{2,1,0:T(8,128)}), f32[2,32,4096]{2,1,0:T(8,128)}) %all-gather.2.cloned.1.call-update) | async-done | bytes 1048592 | tf_op jit(solution)/shard_map/all_gather | solution.py:109
  50.9 1.3 %fusion.41 = (f32[1,32,4096]{2,1,0:T(8,128)S(1)}, f32[1,32,4096]{2,1,0:T(8,128)S(1)}) fusion(f32[2,32,4096]{2,1,0:T(8,128)} %all-gather.2.cloned.1.call-done), kind=kLoop, calls=%fused_computation.109 | loop fusion | bytes 2097152 | tf_op jit(solution)/shard_map/slice | solution.py:98
  53.4 1.9 %sine_bitcast_fusion.1 = (f32[32,8,512]{2,0,1:T(8,128)S(1)}, f32[32,8,512]{2,0,1:T(8,128)S(1)}) fusion(f32[8,32,512]{2,1,0:T(8,128)S(1)} %gather_fusion), kind=kLoop, calls=%fused_computation.49 | loop fusion | bytes 1572864 | tf_op jit(solution)/shard_map/sin | solution.py:89
  56.1 2.2 %multiply_subtract_fusion.1 = (f32[1,1,32,4096]{3,2,1,0:T(8,128)S(1)}, f32[1,1,32,4096]{3,2,1,0:T(8,128)S(1)}) fusion(f32[1,1,32,4096]{3,2,1,0:T(8,128)S(1)} %sin.57, f32[1,1,32,4096]{3,2,1,0:T(8,128)S(1)} %cos.57, f32[4096]{0:T(1024)S(1)} %fusion.24, f32[32]{0:T(128)S(1)} %fusion.29, pred[32]{0:T(512)(128)(4,1)S(1)} %compare_and_fusion), kind=kLoop, calls=%fused_computation.62 | loop fusion | flops 1310720 | bytes 2113696 | tf_op jit(solution)/shard_map/sub | solution.py:90
  58.2 0.9 fusion.13
  59.1 4.6 %collective-permute-start = (f32[2,1,16,4096]{3,2,1,0:T(8,128)}, f32[2,1,16,4096]{3,2,1,0:T(8,128)}, u32[]{:S(2)}, u32[]{:S(2)}) collective-permute-start(f32[2,1,16,4096]{3,2,1,0:T(8,128)} %get-tuple-element.17), channel_id=1, source_target_pairs={{0,1},{1,2},{2,3},{4,5},{5,6},{6,7},{8,9},{9,10},{10,11},{12,13},{... | collective-permute-start | bytes 1572872 | tf_op jit(solution)/shard_map/ppermute | solution.py:20
  63.8 2.1 %collective-permute-start.1 = (f32[2,1,16,4096]{3,2,1,0:T(8,128)S(1)}, f32[2,1,16,4096]{3,2,1,0:T(8,128)}, u32[]{:S(2)}, u32[]{:S(2)}) collective-permute-start(f32[2,1,16,4096]{3,2,1,0:T(8,128)S(1)} %get-tuple-element.18), channel_id=1, source_target_pairs={{1,0},{2,1},{3,2},{5,4},{6,5},{7,6},{9,8},{10,9},{11,10},{13,12},{... | collective-permute-start | bytes 1572872 | tf_op jit(solution)/shard_map/ppermute | solution.py:22
  67.7 1.9 %sine_bitcast_fusion = (f32[32,8,512]{2,0,1:T(8,128)S(1)}, f32[32,8,512]{2,0,1:T(8,128)S(1)}) fusion(f32[8,32,512]{2,1,0:T(8,128)S(1)} %gather_fusion.1), kind=kLoop, calls=%fused_computation.47 | loop fusion | bytes 1572864 | tf_op jit(solution)/shard_map/sin | solution.py:89
  70.4 4.0 %collective-permute-done.1 = f32[2,1,16,4096]{3,2,1,0:T(8,128)} collective-permute-done((f32[2,1,16,4096]{3,2,1,0:T(8,128)S(1)}, f32[2,1,16,4096]{3,2,1,0:T(8,128)}, u32[]{:S(2)}, u32[]{:S(2)}) %collective-permute-start.1) | collective-permute-done | bytes 524320 | tf_op jit(solution)/shard_map/ppermute | solution.py:22
  74.4 1.3 %pad_maximum_fusion = f32[2,1,64,4096]{3,2,1,0:T(8,128)S(1)} fusion(f32[2,1,16,4096]{3,2,1,0:T(8,128)} %collective-permute-done.1, f32[1,1,32,4096]{3,2,1,0:T(8,128)S(1)} %get-tuple-element.12, f32[1,1,32,4096]{3,2,1,0:T(8,128)S(1)} %get-tuple-element.11, f32[2,1,16,4096]{3,2,1,0:T(8,128)} %collective-permute-done), kind=kLoop, calls=%fused_computation.13 | loop fusion | flops 1572864 | bytes 4194304 | tf_op jit(solution)/shard_map/concatenate | solution.py:18
  77.1 0.7 fusion
  78.3 0.7 fusion.1
  79.6 1.0 fusion.11
  80.5 1.0 fusion.10
  81.5 1.8 %convolution_subtract_fusion.3 = f32[32,32,128]{2,1,0:T(8,128)} fusion(f32[32,32,128]{2,1,0:T(8,128)S(1)} %fusion.11, f32[1,32,32,32]{3,2,1,0:T(8,128)S(1)} %bitcast.154, f32[1,32,32,128]{3,2,1,0:T(8,128)S(1)} %bitcast.156, f32[160,128]{1,0:T(8,128)S(1)} %get-tuple-element.6), kind=kOutput, calls=%fused_computation.18 | convolution fusion | flops 251953152 | bytes 1785856 | tf_op jit(solution)/shard_map/...nj,jc->...nc/dot_general | solution.py:64
  83.3 1.1 sub.176
  84.4 1.8 %convolution_add_fusion.3 = f32[32,32,128]{2,1,0:T(8,128)} fusion(f32[32,32,128]{2,1,0:T(8,128)S(1)} %fusion.10, f32[1,32,32,32]{3,2,1,0:T(8,128)S(1)} %bitcast.155, f32[1,32,32,128]{3,2,1,0:T(8,128)S(1)} %bitcast.157, f32[160,128]{1,0:T(8,128)S(1)} %get-tuple-element.5), kind=kOutput, calls=%fused_computation.17 | convolution fusion | flops 251953152 | bytes 1785856 | tf_op jit(solution)/shard_map/...nj,jc->...nc/dot_general | solution.py:64
  86.2 1.1 add.184
  87.5 1.9 %collective-permute-start.2 = (f32[2,1,16,4096]{3,2,1,0:T(8,128)S(1)}, f32[2,1,16,4096]{3,2,1,0:T(8,128)S(1)}, u32[]{:S(2)}, u32[]{:S(2)}) collective-permute-start(f32[2,1,16,4096]{3,2,1,0:T(8,128)S(1)} %get-tuple-element.13), channel_id=1, source_target_pairs={{0,1},{1,2},{2,3},{4,5},{5,6},{6,7},{8,9},{9,10},{10,11},{12,13},{... | collective-permute-start | bytes 1572872 | tf_op jit(solution)/shard_map/ppermute | solution.py:20
  89.5 2.7 %collective-permute-start.3 = (f32[2,1,16,4096]{3,2,1,0:T(8,128)S(1)}, f32[2,1,16,4096]{3,2,1,0:T(8,128)S(1)}, u32[]{:S(2)}, u32[]{:S(2)}) collective-permute-start(f32[2,1,16,4096]{3,2,1,0:T(8,128)S(1)} %get-tuple-element.14), channel_id=1, source_target_pairs={{1,0},{2,1},{3,2},{5,4},{6,5},{7,6},{9,8},{10,9},{11,10},{13,12},{... | collective-permute-start | bytes 1572872 | tf_op jit(solution)/shard_map/ppermute | solution.py:22
  92.1 3.4 %collective-permute-done.2 = f32[2,1,16,4096]{3,2,1,0:T(8,128)S(1)} collective-permute-done((f32[2,1,16,4096]{3,2,1,0:T(8,128)S(1)}, f32[2,1,16,4096]{3,2,1,0:T(8,128)S(1)}, u32[]{:S(2)}, u32[]{:S(2)}) %collective-permute-start.2) | collective-permute-done | bytes 524320 | tf_op jit(solution)/shard_map/ppermute | solution.py:20
  95.6 4.4 %collective-permute-done.3 = f32[2,1,16,4096]{3,2,1,0:T(8,128)S(1)} collective-permute-done((f32[2,1,16,4096]{3,2,1,0:T(8,128)S(1)}, f32[2,1,16,4096]{3,2,1,0:T(8,128)S(1)}, u32[]{:S(2)}, u32[]{:S(2)}) %collective-permute-start.3) | collective-permute-done | bytes 524320 | tf_op jit(solution)/shard_map/ppermute | solution.py:22
  102.8 1.0 fusion.9
  103.7 1.0 fusion.8
  105.9 1.0 convolution_subtract_fusion.2
  107.0 1.0 convolution_add_fusion.2
  108.1 1.0 pad_maximum_fusion.2
  (46 shorter events, 12.2 us)
Async XLA Ops:
  6.5 44.3 %all-gather.2.cloned.1.call-start = ((), (), s32[]{:S(2)}) async-start(), calls=%async_computation | async-start | bytes 1179648 | tf_op jit(solution)/shard_map/all_gather | solution.py:109
  59.1 11.3 %collective-permute-start = (f32[2,1,16,4096]{3,2,1,0:T(8,128)}, f32[2,1,16,4096]{3,2,1,0:T(8,128)}, u32[]{:S(2)}, u32[]{:S(2)}) collective-permute-start(f32[2,1,16,4096]{3,2,1,0:T(8,128)} %get-tuple-element.17), channel_id=1, source_target_pairs={{0,1},{1,2},{2,3},{4,5},{5,6},{6,7},{8,9},{9,10},{10,11},{12,13},{... | collective-permute-start | bytes 1572872 | tf_op jit(solution)/shard_map/ppermute | solution.py:20
  63.8 10.6 %collective-permute-start.1 = (f32[2,1,16,4096]{3,2,1,0:T(8,128)S(1)}, f32[2,1,16,4096]{3,2,1,0:T(8,128)}, u32[]{:S(2)}, u32[]{:S(2)}) collective-permute-start(f32[2,1,16,4096]{3,2,1,0:T(8,128)S(1)} %get-tuple-element.18), channel_id=1, source_target_pairs={{1,0},{2,1},{3,2},{5,4},{6,5},{7,6},{9,8},{10,9},{11,10},{13,12},{... | collective-permute-start | bytes 1572872 | tf_op jit(solution)/shard_map/ppermute | solution.py:22
  87.5 8.0 %collective-permute-start.2 = (f32[2,1,16,4096]{3,2,1,0:T(8,128)S(1)}, f32[2,1,16,4096]{3,2,1,0:T(8,128)S(1)}, u32[]{:S(2)}, u32[]{:S(2)}) collective-permute-start(f32[2,1,16,4096]{3,2,1,0:T(8,128)S(1)} %get-tuple-element.13), channel_id=1, source_target_pairs={{0,1},{1,2},{2,3},{4,5},{5,6},{6,7},{8,9},{9,10},{10,11},{12,13},{... | collective-permute-start | bytes 1572872 | tf_op jit(solution)/shard_map/ppermute | solution.py:20
  89.5 10.5 %collective-permute-start.3 = (f32[2,1,16,4096]{3,2,1,0:T(8,128)S(1)}, f32[2,1,16,4096]{3,2,1,0:T(8,128)S(1)}, u32[]{:S(2)}, u32[]{:S(2)}) collective-permute-start(f32[2,1,16,4096]{3,2,1,0:T(8,128)S(1)} %get-tuple-element.14), channel_id=1, source_target_pairs={{1,0},{2,1},{3,2},{5,4},{6,5},{7,6},{9,8},{10,9},{11,10},{13,12},{... | collective-permute-start | bytes 1572872 | tf_op jit(solution)/shard_map/ppermute | solution.py:22
Sparse Core Ops, SparseCore 0:
  9.5 41.2 all-gather.1
where the time goes:
time: 116 us
  waiting for transfers between devices  51.6 us (44%)
  local copies, waits for them, and re-layouts  15.7 us (14%)
  matrix products  14.8 us (13%)
  between operations  13.8 us (12%)
  starting transfers between devices  11.3 us (10%)
  other arithmetic  8.69 us (7%)
    all_gather x1, waiting for transfers between devices, body(): gathered = lax.all_gather(stored_planes, 'illum', axis=2, tiled=True)  39.1 us
    dot_general x8, matrix products, apply(): jnp.einsum('...nj,jc->...nc', win, kern, precision=lax.Precision.HIGHEST)  9.36 us
    ppermute x2, waiting for transfers between devices, extended(): lax.ppermute(head, axis, [((i + 1) % count, i) for i in range(ends)])  8.37 us
    ppermute x2, starting transfers between devices, extended(): lax.ppermute(tail, axis, [(i, (i + 1) % count) for i in range(ends)])  6.56 us
    dot_general x8, matrix products, apply(): jnp.einsum('ij,ajy->aiy', band, field, precision=lax.Precision.HIGHEST)  5.44 us
    ppermute x2, starting transfers between devices, extended(): lax.ppermute(head, axis, [((i + 1) % count, i) for i in range(ends)])  4.76 us
    sin x6, local copies, waits for them, and re-layouts, transmit(): sine = jnp.sin(screen)  4.53 us
    ppermute x2, waiting for transfers between devices, extended(): lax.ppermute(tail, axis, [(i, (i + 1) % count) for i in range(ends)])  3.44 us
  transfers between devices with their start and end apart: 5, of which 4 were waited for; matrix products, arithmetic and copies ran while one was open for 8% of the time, Pallas kernels for 0%

commit v1 on v0

--- a/solution.py
+++ b/solution.py
@@ -7,6 +7,13 @@
 PLANES = 2
 HALF = 16
 two_pi = 6.283185307179586
+
+
+def kinds_extend(u, axis_no):
+    carry_in = list(u.shape[1:])
+    carry_in[axis_no] *= u.shape[0]
+    y_new = jnp.moveaxis(u, 0, axis_no).reshape(carry_in)
+    return y_new
 
 
 def extended(cells, sides, width):
@@ -106,7 +113,24 @@
     total_rows = local_rows * lax.axis_size("tile")
     total_cols = NY
     first_row = lax.axis_index("tile") * local_rows
-    gathered = lax.all_gather(stored_planes, "illum", axis=2, tiled=True)
+    amount_of = lax.psum(1, "illum")
+    history = [(s, (s + 1) % amount_of) for s in range(amount_of)]
+    slots = [(hop_no, num) for num, hop_no in history]
+    wide_out, state_now = ([], [])
+    for idx in [*range(amount_of - 1)]:
+        if idx % 2 == 0:
+            front = lax.ppermute(wide_out[-1] if wide_out else stored_planes, "illum", history)
+            wide_out.append(front)
+        else:
+            state_now.append(
+                lax.ppermute(state_now[-1] if state_now else stored_planes, "illum", slots)
+            )
+    all_rows = jnp.stack([*wide_out[::-1], stored_planes, *state_now])
+    everything = lax.axis_index("illum")
+    x_new = len(wide_out)
+    passed = everything - x_new
+    all_rows = all_rows[(jnp.arange(amount_of) - passed) % amount_of]
+    gathered = kinds_extend(all_rows, 2)
     screens = reorder(gathered, owner)
     extra = 0
     span = local_rows + 2 * extra

time: 116 us -> 89.5 us (0.77)
  waiting for transfers between devices: 51.6 us -> 20.2 us
  starting transfers between devices: 11.3 us -> 29.7 us
  between operations: 13.8 us -> 0.49 us
    all_gather x1 -> x0, waiting for transfers between devices: 39.1 us -> none  [body(): gathered = lax.all_gather(stored_planes, 'illum', axis=2, tiled=True)]
    ppermute x0 -> x7, starting transfers between devices: none -> 14 us  [the longest x3 11.9 us: body(): lax.ppermute(state_now[-1] if state_now else stored_planes, 'illum', slots)]
    ppermute x0 -> x7, waiting for transfers between devices: none -> 9.75 us  [the longest x4 9.06 us: body(): lax.ppermute(wide_out[-1] if wide_out else stored_planes, 'illum', history)]
    ppermute x2, starting transfers between devices: 6.56 us -> 11.6 us  [extended(): lax.ppermute(tail, axis, [(i, (i + 1) % count) for i in range(ends)])]
    ppermute x2, waiting for transfers between devices: 3.44 us -> 1.61 us  [extended(): lax.ppermute(tail, axis, [(i, (i + 1) % count) for i in range(ends)])]
    slice x1 -> x0, local copies, waits for them, and re-layouts: 1.27 us -> none  [reorder(): gathered[p].reshape(count, blocks, width)[:, owner[p], :]]
    unnamed x14 -> x19, local copies, waits for them, and re-layouts: 2.72 us -> 3.09 us
  transfers between devices with their start and end apart: 5 -> 11, of which waited for: 4 -> 9; matrix products, arithmetic and copies ran while one was open for 8% -> 10% of each run, Pallas kernels for 0% -> 0%
where the time goes in v1:
time: 89.5 us; the launch traced here: 88.7 us
  starting transfers between devices  29.7 us (33%)
  waiting for transfers between devices  20.2 us (23%)
  local copies, waits for them, and re-layouts  14.9 us (17%)
  matrix products  14.8 us (17%)
  other arithmetic  8.65 us (10%)
    ppermute x3, starting transfers between devices, body(): lax.ppermute(state_now[-1] if state_now else stored_planes, 'illum', slots)  11.9 us
    ppermute x2, starting transfers between devices, extended(): lax.ppermute(tail, axis, [(i, (i + 1) % count) for i in range(ends)])  11.6 us
    dot_general x8, matrix products, apply(): jnp.einsum('...nj,jc->...nc', win, kern, precision=lax.Precision.HIGHEST)  9.37 us
    ppermute x4, waiting for transfers between devices, body(): lax.ppermute(wide_out[-1] if wide_out else stored_planes, 'illum', history)  9.06 us
    ppermute x2, waiting for transfers between devices, extended(): lax.ppermute(head, axis, [((i + 1) % count, i) for i in range(ends)])  8.89 us
    dot_general x8, matrix products, apply(): jnp.einsum('ij,ajy->aiy', band, field, precision=lax.Precision.HIGHEST)  5.44 us
    sin x6, local copies, waits for them, and re-layouts, transmit(): sine = jnp.sin(screen)  4.53 us
    ppermute x2, starting transfers between devices, extended(): lax.ppermute(head, axis, [((i + 1) % count, i) for i in range(ends)])  4.02 us
  transfers between devices with their start and end apart: 11, of which 9 were waited for; matrix products, arithmetic and copies ran while one was open for 10% of the time, Pallas kernels for 0%

profile of v1, /device:TPU:1, one launch (start us, length us, event | category | flops | bytes accessed | tf_op | source)
XLA Modules:
  0.0 88.7 jit_solution(4689435248343151030)
XLA Ops:
  0.0 2.1 %collective-permute-start = (f32[2,32,512]{2,1,0:T(8,128)}, f32[2,32,512]{2,1,0:T(8,128)S(1)}, u32[]{:S(2)}, u32[]{:S(2)}) collective-permute-start(f32[2,32,512]{2,1,0:T(8,128)} %param.6), channel_id=1, source_target_pairs={{0,4},{4,8},{8,12},{12,16},{16,20},{20,24},{24,28},{28,0},{1,5},{5... | collective-permute-start | bytes 393224 | tf_op jit(solution)/shard_map/ppermute | solution.py:122
  2.1 3.0 %collective-permute-start.4 = (f32[2,32,512]{2,1,0:T(8,128)}, f32[2,32,512]{2,1,0:T(8,128)S(1)}, u32[]{:S(2)}, u32[]{:S(2)}) collective-permute-start(f32[2,32,512]{2,1,0:T(8,128)} %param.6), channel_id=1, source_target_pairs={{4,0},{8,4},{12,8},{16,12},{20,16},{24,20},{28,24},{0,28},{5,1},{9... | collective-permute-start | bytes 393224 | tf_op jit(solution)/shard_map/ppermute | solution.py:126
  5.9 1.3 %fusion.43 = (s32[1,1]{1,0:T(1,128)}, s32[1,1]{1,0:T(1,128)}) fusion(s32[1,2]{1,0:T(1,128)} %param.4), kind=kLoop, calls=%fused_computation.127 | loop fusion | bytes 16 | tf_op jit(solution)/shard_map/slice | solution.py:141
  8.6 6.5 %collective-permute-done.1 = f32[2,32,512]{2,1,0:T(8,128)S(1)} collective-permute-done((f32[2,32,512]{2,1,0:T(8,128)S(1)}, f32[2,32,512]{2,1,0:T(8,128)S(1)}, u32[]{:S(2)}, u32[]{:S(2)}) %collective-permute-start.1) | collective-permute-done | bytes 131104 | tf_op jit(solution)/shard_map/ppermute | solution.py:122
  16.4 4.2 %collective-permute-start.5 = (f32[2,32,512]{2,1,0:T(8,128)S(1)}, f32[2,32,512]{2,1,0:T(8,128)S(1)}, u32[]{:S(2)}, u32[]{:S(2)}) collective-permute-start(f32[2,32,512]{2,1,0:T(8,128)S(1)} %collective-permute-done.4), channel_id=1, source_target_pairs={{4,0},{8,4},{12,8},{16,12},{20,16},{24,20},{28,24},{0,28},{5,1},{9... | collective-permute-start | bytes 393224 | tf_op jit(solution)/shard_map/ppermute | solution.py:126
  20.6 1.1 %collective-permute-done.2 = f32[2,32,512]{2,1,0:T(8,128)S(1)} collective-permute-done((f32[2,32,512]{2,1,0:T(8,128)S(1)}, f32[2,32,512]{2,1,0:T(8,128)S(1)}, u32[]{:S(2)}, u32[]{:S(2)}) %collective-permute-start.2) | collective-permute-done | bytes 131104 | tf_op jit(solution)/shard_map/ppermute | solution.py:122
  22.5 4.7 %collective-permute-start.6 = (f32[2,32,512]{2,1,0:T(8,128)S(1)}, f32[2,32,512]{2,1,0:T(8,128)S(1)}, u32[]{:S(2)}, u32[]{:S(2)}) collective-permute-start(f32[2,32,512]{2,1,0:T(8,128)S(1)} %collective-permute-done.5), channel_id=1, source_target_pairs={{4,0},{8,4},{12,8},{16,12},{20,16},{24,20},{28,24},{0,28},{5,1},{9... | collective-permute-start | bytes 393224 | tf_op jit(solution)/shard_map/ppermute | solution.py:126
  27.2 1.0 %collective-permute-done.3 = f32[2,32,512]{2,1,0:T(8,128)S(1)} collective-permute-done((f32[2,32,512]{2,1,0:T(8,128)S(1)}, f32[2,32,512]{2,1,0:T(8,128)S(1)}, u32[]{:S(2)}, u32[]{:S(2)}) %collective-permute-start.3) | collective-permute-done | bytes 131104 | tf_op jit(solution)/shard_map/ppermute | solution.py:122
  28.2 0.9 %bitcast_dynamic-update-slice_fusion.3 = f32[8,2,32,512]{3,2,1,0:T(8,128)S(1)} fusion(f32[8,2,32,512]{3,2,1,0:T(8,128)S(1)} %bitcast_dynamic-update-slice_fusion.4, f32[2,32,512]{2,1,0:T(8,128)} %param.6), kind=kLoop, calls=%fused_computation.72 | loop fusion | bytes 262144
  30.5 1.9 %sine_bitcast_fusion.1 = (f32[32,8,512]{2,0,1:T(8,128)S(1)}, f32[32,8,512]{2,0,1:T(8,128)S(1)}) fusion(f32[8,32,512]{2,1,0:T(8,128)S(1)} %gather_fusion.1), kind=kLoop, calls=%fused_computation.52 | loop fusion | bytes 1572864 | tf_op jit(solution)/shard_map/sin | solution.py:96
  33.3 2.2 %multiply_subtract_fusion.1 = (f32[1,1,32,4096]{3,2,1,0:T(8,128)S(1)}, f32[1,1,32,4096]{3,2,1,0:T(8,128)S(1)}) fusion(f32[1,1,32,4096]{3,2,1,0:T(8,128)S(1)} %sin.57, f32[1,1,32,4096]{3,2,1,0:T(8,128)S(1)} %cos.57, f32[4096]{0:T(1024)S(1)} %fusion.24, f32[32]{0:T(128)S(1)} %fusion.29, pred[32]{0:T(512)(128)(4,1)S(1)} %compare_and_fusion), kind=kLoop, calls=%fused_computation.65 | loop fusion | flops 1310720 | bytes 2113696 | tf_op jit(solution)/shard_map/sub | solution.py:97
  35.4 0.9 fusion.13
  36.3 7.8 %collective-permute-start.7 = (f32[2,1,16,4096]{3,2,1,0:T(8,128)}, f32[2,1,16,4096]{3,2,1,0:T(8,128)}, u32[]{:S(2)}, u32[]{:S(2)}) collective-permute-start(f32[2,1,16,4096]{3,2,1,0:T(8,128)} %get-tuple-element.17), channel_id=1, source_target_pairs={{0,1},{1,2},{2,3},{4,5},{5,6},{6,7},{8,9},{9,10},{10,11},{12,13},{... | collective-permute-start | bytes 1572872 | tf_op jit(solution)/shard_map/ppermute | solution.py:27
  44.1 2.1 %collective-permute-start.8 = (f32[2,1,16,4096]{3,2,1,0:T(8,128)S(1)}, f32[2,1,16,4096]{3,2,1,0:T(8,128)}, u32[]{:S(2)}, u32[]{:S(2)}) collective-permute-start(f32[2,1,16,4096]{3,2,1,0:T(8,128)S(1)} %get-tuple-element.18), channel_id=1, source_target_pairs={{1,0},{2,1},{3,2},{5,4},{6,5},{7,6},{9,8},{10,9},{11,10},{13,12},{... | collective-permute-start | bytes 1572872 | tf_op jit(solution)/shard_map/ppermute | solution.py:29
  47.4 1.9 %sine_bitcast_fusion = (f32[32,8,512]{2,0,1:T(8,128)S(1)}, f32[32,8,512]{2,0,1:T(8,128)S(1)}) fusion(f32[8,32,512]{2,1,0:T(8,128)S(1)} %gather_fusion.2), kind=kLoop, calls=%fused_computation.50 | loop fusion | bytes 1572864 | tf_op jit(solution)/shard_map/sin | solution.py:96
  50.5 4.2 %collective-permute-done.8 = f32[2,1,16,4096]{3,2,1,0:T(8,128)} collective-permute-done((f32[2,1,16,4096]{3,2,1,0:T(8,128)S(1)}, f32[2,1,16,4096]{3,2,1,0:T(8,128)}, u32[]{:S(2)}, u32[]{:S(2)}) %collective-permute-start.8) | collective-permute-done | bytes 524320 | tf_op jit(solution)/shard_map/ppermute | solution.py:29
  54.7 1.3 %pad_maximum_fusion = f32[2,1,64,4096]{3,2,1,0:T(8,128)S(1)} fusion(f32[2,1,16,4096]{3,2,1,0:T(8,128)} %collective-permute-done.8, f32[1,1,32,4096]{3,2,1,0:T(8,128)S(1)} %get-tuple-element.12, f32[1,1,32,4096]{3,2,1,0:T(8,128)S(1)} %get-tuple-element.11, f32[2,1,16,4096]{3,2,1,0:T(8,128)} %collective-permute-done.7), kind=kLoop, calls=%fused_computation.14 | loop fusion | flops 1572864 | bytes 4194304 | tf_op jit(solution)/shard_map/concatenate | solution.py:25
  59.9 1.0 %fusion.11 = f32[32,32,128]{2,1,0:T(8,128)S(1)} fusion(f32[1,32,32,32]{3,2,1,0:T(8,128)S(1)} %bitcast.163, f32[1,32,32,128]{3,2,1,0:T(8,128)S(1)} %bitcast.165, f32[160,128]{1,0:T(8,128)S(1)} %get-tuple-element.5), kind=kOutput, calls=%fused_computation.40 | convolution fusion | flops 251822080 | bytes 1261568 | tf_op jit(solution)/shard_map/...nj,jc->...nc/dot_general | solution.py:71
  60.9 1.0 %fusion.10 = f32[32,32,128]{2,1,0:T(8,128)S(1)} fusion(f32[1,32,32,32]{3,2,1,0:T(8,128)S(1)} %bitcast.164, f32[1,32,32,128]{3,2,1,0:T(8,128)S(1)} %bitcast.166, f32[160,128]{1,0:T(8,128)S(1)} %get-tuple-element.6), kind=kOutput, calls=%fused_computation.39 | convolution fusion | flops 251822080 | bytes 1261568 | tf_op jit(solution)/shard_map/...nj,jc->...nc/dot_general | solution.py:71
  61.8 1.8 %convolution_subtract_fusion.3 = f32[32,32,128]{2,1,0:T(8,128)} fusion(f32[32,32,128]{2,1,0:T(8,128)S(1)} %fusion.11, f32[1,32,32,32]{3,2,1,0:T(8,128)S(1)} %bitcast.171, f32[1,32,32,128]{3,2,1,0:T(8,128)S(1)} %bitcast.173, f32[160,128]{1,0:T(8,128)S(1)} %get-tuple-element.6), kind=kOutput, calls=%fused_computation.19 | convolution fusion | flops 251953152 | bytes 1785856 | tf_op jit(solution)/shard_map/...nj,jc->...nc/dot_general | solution.py:71
  63.6 1.1 %sub.195 = f32[1,1,32,4096]{3,2,1,0:T(8,128)S(1)} reshape(f32[32,32,128]{2,1,0:T(8,128)} %convolution_subtract_fusion.3) | data formatting | bytes 1048576 | tf_op jit(solution)/shard_map/sub | solution.py:75
  64.7 1.8 %convolution_add_fusion.3 = f32[32,32,128]{2,1,0:T(8,128)} fusion(f32[32,32,128]{2,1,0:T(8,128)S(1)} %fusion.10, f32[1,32,32,32]{3,2,1,0:T(8,128)S(1)} %bitcast.172, f32[1,32,32,128]{3,2,1,0:T(8,128)S(1)} %bitcast.174, f32[160,128]{1,0:T(8,128)S(1)} %get-tuple-element.5), kind=kOutput, calls=%fused_computation.18 | convolution fusion | flops 251953152 | bytes 1785856 | tf_op jit(solution)/shard_map/...nj,jc->...nc/dot_general | solution.py:71
  66.5 1.1 %add.210 = f32[1,1,32,4096]{3,2,1,0:T(8,128)S(1)} reshape(f32[32,32,128]{2,1,0:T(8,128)} %convolution_add_fusion.3) | data formatting | bytes 1048576 | tf_op jit(solution)/shard_map/add | solution.py:76
  67.9 1.9 %collective-permute-start.10 = (f32[2,1,16,4096]{3,2,1,0:T(8,128)S(1)}, f32[2,1,16,4096]{3,2,1,0:T(8,128)S(1)}, u32[]{:S(2)}, u32[]{:S(2)}) collective-permute-start(f32[2,1,16,4096]{3,2,1,0:T(8,128)S(1)} %get-tuple-element.14), channel_id=1, source_target_pairs={{1,0},{2,1},{3,2},{5,4},{6,5},{7,6},{9,8},{10,9},{11,10},{13,12},{... | collective-permute-start | bytes 1572872 | tf_op jit(solution)/shard_map/ppermute | solution.py:29
  69.8 3.9 %collective-permute-start.9 = (f32[2,1,16,4096]{3,2,1,0:T(8,128)S(1)}, f32[2,1,16,4096]{3,2,1,0:T(8,128)S(1)}, u32[]{:S(2)}, u32[]{:S(2)}) collective-permute-start(f32[2,1,16,4096]{3,2,1,0:T(8,128)S(1)} %get-tuple-element.13), channel_id=1, source_target_pairs={{0,1},{1,2},{2,3},{4,5},{5,6},{6,7},{8,9},{9,10},{10,11},{12,13},{... | collective-permute-start | bytes 1572872 | tf_op jit(solution)/shard_map/ppermute | solution.py:27
  73.7 4.7 %collective-permute-done.10 = f32[2,1,16,4096]{3,2,1,0:T(8,128)S(1)} collective-permute-done((f32[2,1,16,4096]{3,2,1,0:T(8,128)S(1)}, f32[2,1,16,4096]{3,2,1,0:T(8,128)S(1)}, u32[]{:S(2)}, u32[]{:S(2)}) %collective-permute-start.10) | collective-permute-done | bytes 524320 | tf_op jit(solution)/shard_map/ppermute | solution.py:29
  78.4 1.2 %collective-permute-done.9 = f32[2,1,16,4096]{3,2,1,0:T(8,128)S(1)} collective-permute-done((f32[2,1,16,4096]{3,2,1,0:T(8,128)S(1)}, f32[2,1,16,4096]{3,2,1,0:T(8,128)S(1)}, u32[]{:S(2)}, u32[]{:S(2)}) %collective-permute-start.9) | collective-permute-done | bytes 524320 | tf_op jit(solution)/shard_map/ppermute | solution.py:27
  82.3 1.0 %fusion.9 = f32[32,32,128]{2,1,0:T(8,128)S(1)} fusion(f32[1,32,32,32]{3,2,1,0:T(8,128)S(1)} %bitcast.167, f32[1,32,32,128]{3,2,1,0:T(8,128)S(1)} %bitcast.169, f32[160,128]{1,0:T(8,128)S(1)} %get-tuple-element.5), kind=kOutput, calls=%fused_computation.38 | convolution fusion | flops 251822080 | bytes 1261568 | tf_op jit(solution)/shard_map/...nj,jc->...nc/dot_general | solution.py:71
  83.3 1.0 %fusion.8 = f32[32,32,128]{2,1,0:T(8,128)S(1)} fusion(f32[1,32,32,32]{3,2,1,0:T(8,128)S(1)} %bitcast.168, f32[1,32,32,128]{3,2,1,0:T(8,128)S(1)} %bitcast.170, f32[160,128]{1,0:T(8,128)S(1)} %get-tuple-element.6), kind=kOutput, calls=%fused_computation.37 | convolution fusion | flops 251822080 | bytes 1261568 | tf_op jit(solution)/shard_map/...nj,jc->...nc/dot_general | solution.py:71
  85.5 1.0 %convolution_subtract_fusion.2 = f32[32,32,128]{2,1,0:T(8,128)S(1)} fusion(f32[32,32,128]{2,1,0:T(8,128)S(1)} %fusion.9, f32[1,32,32,32]{3,2,1,0:T(8,128)S(1)} %bitcast.175, f32[1,32,32,128]{3,2,1,0:T(8,128)S(1)} %bitcast.177, f32[160,128]{1,0:T(8,128)S(1)} %get-tuple-element.6), kind=kOutput, calls=%fused_computation.17 | convolution fusion | flops 251953152 | bytes 1785856 | tf_op jit(solution)/shard_map/...nj,jc->...nc/dot_general | solution.py:71
  86.6 1.0 %convolution_add_fusion.2 = f32[32,32,128]{2,1,0:T(8,128)S(1)} fusion(f32[32,32,128]{2,1,0:T(8,128)S(1)} %fusion.8, f32[1,32,32,32]{3,2,1,0:T(8,128)S(1)} %bitcast.176, f32[1,32,32,128]{3,2,1,0:T(8,128)S(1)} %bitcast.178, f32[160,128]{1,0:T(8,128)S(1)} %get-tuple-element.5), kind=kOutput, calls=%fused_computation.16 | convolution fusion | flops 251953152 | bytes 1785856 | tf_op jit(solution)/shard_map/...nj,jc->...nc/dot_general | solution.py:71
  87.7 1.0 %pad_maximum_fusion.2 = f32[2,1,32,4096]{3,2,1,0:T(8,128)} fusion(f32[1,1,32,4096]{3,2,1,0:T(8,128)S(1)} %add.216, f32[1,1,32,4096]{3,2,1,0:T(8,128)S(1)} %sub.201), kind=kLoop, calls=%fused_computation.32 | loop fusion | flops 262144 | bytes 2097152 | tf_op jit(solution)/shard_map/stack | solution.py:152
  (64 shorter events, 17.0 us)
Async XLA Ops:
  0.0 8.5 %collective-permute-start = (f32[2,32,512]{2,1,0:T(8,128)}, f32[2,32,512]{2,1,0:T(8,128)S(1)}, u32[]{:S(2)}, u32[]{:S(2)}) collective-permute-start(f32[2,32,512]{2,1,0:T(8,128)} %param.6), channel_id=1, source_target_pairs={{0,4},{4,8},{8,12},{12,16},{16,20},{20,24},{24,28},{28,0},{1,5},{5... | collective-permute-start | bytes 393224 | tf_op jit(solution)/shard_map/ppermute | solution.py:122
  2.1 14.3 %collective-permute-start.4 = (f32[2,32,512]{2,1,0:T(8,128)}, f32[2,32,512]{2,1,0:T(8,128)S(1)}, u32[]{:S(2)}, u32[]{:S(2)}) collective-permute-start(f32[2,32,512]{2,1,0:T(8,128)} %param.6), channel_id=1, source_target_pairs={{4,0},{8,4},{12,8},{16,12},{20,16},{24,20},{28,24},{0,28},{5,1},{9... | collective-permute-start | bytes 393224 | tf_op jit(solution)/shard_map/ppermute | solution.py:126
  8.5 6.5 %collective-permute-start.1 = (f32[2,32,512]{2,1,0:T(8,128)S(1)}, f32[2,32,512]{2,1,0:T(8,128)S(1)}, u32[]{:S(2)}, u32[]{:S(2)}) collective-permute-start(f32[2,32,512]{2,1,0:T(8,128)S(1)} %collective-permute-done), channel_id=1, source_target_pairs={{0,4},{4,8},{8,12},{12,16},{16,20},{20,24},{24,28},{28,0},{1,5},{5... | collective-permute-start | bytes 393224 | tf_op jit(solution)/shard_map/ppermute | solution.py:122
  15.1 6.6 %collective-permute-start.2 = (f32[2,32,512]{2,1,0:T(8,128)S(1)}, f32[2,32,512]{2,1,0:T(8,128)S(1)}, u32[]{:S(2)}, u32[]{:S(2)}) collective-permute-start(f32[2,32,512]{2,1,0:T(8,128)S(1)} %collective-permute-done.1), channel_id=1, source_target_pairs={{0,4},{4,8},{8,12},{12,16},{16,20},{20,24},{24,28},{28,0},{1,5},{5... | collective-permute-start | bytes 393224 | tf_op jit(solution)/shard_map/ppermute | solution.py:122
  16.4 6.2 %collective-permute-start.5 = (f32[2,32,512]{2,1,0:T(8,128)S(1)}, f32[2,32,512]{2,1,0:T(8,128)S(1)}, u32[]{:S(2)}, u32[]{:S(2)}) collective-permute-start(f32[2,32,512]{2,1,0:T(8,128)S(1)} %collective-permute-done.4), channel_id=1, source_target_pairs={{4,0},{8,4},{12,8},{16,12},{20,16},{24,20},{28,24},{0,28},{5,1},{9... | collective-permute-start | bytes 393224 | tf_op jit(solution)/shard_map/ppermute | solution.py:126
  21.7 6.5 %collective-permute-start.3 = (f32[2,32,512]{2,1,0:T(8,128)S(1)}, f32[2,32,512]{2,1,0:T(8,128)S(1)}, u32[]{:S(2)}, u32[]{:S(2)}) collective-permute-start(f32[2,32,512]{2,1,0:T(8,128)S(1)} %collective-permute-done.2), channel_id=1, source_target_pairs={{0,4},{4,8},{8,12},{12,16},{16,20},{20,24},{24,28},{28,0},{1,5},{5... | collective-permute-start | bytes 393224 | tf_op jit(solution)/shard_map/ppermute | solution.py:122
  22.5 6.7 %collective-permute-start.6 = (f32[2,32,512]{2,1,0:T(8,128)S(1)}, f32[2,32,512]{2,1,0:T(8,128)S(1)}, u32[]{:S(2)}, u32[]{:S(2)}) collective-permute-start(f32[2,32,512]{2,1,0:T(8,128)S(1)} %collective-permute-done.5), channel_id=1, source_target_pairs={{4,0},{8,4},{12,8},{16,12},{20,16},{24,20},{28,24},{0,28},{5,1},{9... | collective-permute-start | bytes 393224 | tf_op jit(solution)/shard_map/ppermute | solution.py:126
  36.3 14.2 %collective-permute-start.7 = (f32[2,1,16,4096]{3,2,1,0:T(8,128)}, f32[2,1,16,4096]{3,2,1,0:T(8,128)}, u32[]{:S(2)}, u32[]{:S(2)}) collective-permute-start(f32[2,1,16,4096]{3,2,1,0:T(8,128)} %get-tuple-element.17), channel_id=1, source_target_pairs={{0,1},{1,2},{2,3},{4,5},{5,6},{6,7},{8,9},{9,10},{10,11},{12,13},{... | collective-permute-start | bytes 1572872 | tf_op jit(solution)/shard_map/ppermute | solution.py:27
  44.1 10.6 %collective-permute-start.8 = (f32[2,1,16,4096]{3,2,1,0:T(8,128)S(1)}, f32[2,1,16,4096]{3,2,1,0:T(8,128)}, u32[]{:S(2)}, u32[]{:S(2)}) collective-permute-start(f32[2,1,16,4096]{3,2,1,0:T(8,128)S(1)} %get-tuple-element.18), channel_id=1, source_target_pairs={{1,0},{2,1},{3,2},{5,4},{6,5},{7,6},{9,8},{10,9},{11,10},{13,12},{... | collective-permute-start | bytes 1572872 | tf_op jit(solution)/shard_map/ppermute | solution.py:29
  67.9 10.5 %collective-permute-start.10 = (f32[2,1,16,4096]{3,2,1,0:T(8,128)S(1)}, f32[2,1,16,4096]{3,2,1,0:T(8,128)S(1)}, u32[]{:S(2)}, u32[]{:S(2)}) collective-permute-start(f32[2,1,16,4096]{3,2,1,0:T(8,128)S(1)} %get-tuple-element.14), channel_id=1, source_target_pairs={{1,0},{2,1},{3,2},{5,4},{6,5},{7,6},{9,8},{10,9},{11,10},{13,12},{... | collective-permute-start | bytes 1572872 | tf_op jit(solution)/shard_map/ppermute | solution.py:29
  69.8 9.8 %collective-permute-start.9 = (f32[2,1,16,4096]{3,2,1,0:T(8,128)S(1)}, f32[2,1,16,4096]{3,2,1,0:T(8,128)S(1)}, u32[]{:S(2)}, u32[]{:S(2)}) collective-permute-start(f32[2,1,16,4096]{3,2,1,0:T(8,128)S(1)} %get-tuple-element.13), channel_id=1, source_target_pairs={{0,1},{1,2},{2,3},{4,5},{5,6},{6,7},{8,9},{9,10},{10,11},{12,13},{... | collective-permute-start | bytes 1572872 | tf_op jit(solution)/shard_map/ppermute | solution.py:27
